TPU v7x, 256 devices: a whole 4x4x8 slice. The times are simulated.
256 devices in a mesh: tm: 32 (over y, z_hi, core), rows: 8 (over z_lo, x).
Axes of the slice: x: 4, y: 4, z: 8 (z_hi: 4, z_lo: 2; z = z_hi * 2 + z_lo), core: 2. Of those that a mesh axis runs over, the one named last changes fastest.
Arguments:
- latent: bfloat16 [32, 16, 128, 512], P('tm', 'rows'), may hold values from -32 to 32
- norm_gain: float32 [512], replicated, may hold values from 0.1 to 1.9
- conv_weight: bfloat16 [27, 512, 512], P(None, 'tm'), may hold values from -0.0546875 to 0.0546875
- grad_out: bfloat16 [32, 16, 128, 512], P('tm', 'rows'), may hold values from -6 to 6
Outputs:
- refined: bfloat16 [32, 16, 128, 512], P('tm', 'rows')
- grad_latent: float32 [32, 16, 128, 512], P('tm', 'rows')
All inputs are finite; a program needn't handle non-finite values.
Results may differ from a plain program's by a relative error of at most 0.0013.
The roundings to bfloat16 on the way count: a program that leaves them out, or rounds other values in their place, can miss the bound.
Values may be sent and summed in bfloat16 or wider, within the bound.
No kernel may reach another device: no remote copies, remote signals or barrier semaphores. Data moves between devices by JAX's collectives and lax.ppermute only.
A program may use at most 64 MiB of HBM per device.

v0:
```python
import jax
import jax.numpy as jnp
from jax import lax
from jax.sharding import PartitionSpec as P

GROUPS = 32
epsilon = 1e-06


def shifted(block, axis, distance):
    devices = range(lax.axis_size(axis))
    route = [(i - distance, i) for i in devices if i - distance in devices]
    return lax.ppermute(block, axis, route)


def with_halo(shard, sides, width):
    for axis, dim in sides:
        size, length = (lax.axis_size(axis), shard.shape[dim])
        up = [(i, (i + 1) % size) for i in range(size - 1)]
        down = [(j, i) for i, j in up]
        last = lax.slice_in_dim(shard, length - width, length, axis=dim)
        first = lax.slice_in_dim(shard, 0, width, axis=dim)
        before = lax.ppermute(last, axis, up)
        after = lax.ppermute(first, axis, down)
        shard = jnp.concatenate([before, shard, after], axis=dim)
    return shard


def grouped_view(values):
    return values.reshape(
        values.shape[0], values.shape[1] * values.shape[2], GROUPS, values.shape[3] // GROUPS
    )


def widen_columns(values):
    return jnp.pad(values, ((0, 0), (0, 0), (1, 1), (0, 0)))


def shards(latent, norm_gain, conv_weight, grad_out):
    frames_here, rows_here, columns, channels = latent.shape
    cell_count = lax.axis_size("rows") * rows_here * columns * (channels // GROUPS)
    full_weight = lax.all_gather(conv_weight, "tm", axis=1, tiled=True)
    latent_wide = latent.astype(jnp.float32)
    grouped = grouped_view(latent_wide)
    average = lax.psum(jnp.sum(grouped, axis=(1, 3)), "rows") / cell_count
    centred = grouped - average[:, None, :, None]
    spread = lax.psum(jnp.sum(centred * centred, axis=(1, 3)), "rows") / cell_count
    inverse = lax.rsqrt(spread + epsilon)
    normed_grouped = centred * inverse[:, None, :, None]
    normed = normed_grouped.reshape(latent.shape)
    scaled = normed * norm_gain
    sigmoid_value = jax.nn.sigmoid(scaled)
    activated = (scaled * sigmoid_value).astype(jnp.bfloat16)
    before_one = shifted(activated, "tm", 1)
    before_two = shifted(activated, "tm", 2)
    padded = with_halo(
        jnp.concatenate([before_two, before_one, activated], axis=0), (("rows", 1),), 1
    )
    after_one = shifted(grad_out, "tm", -1)
    after_two = shifted(grad_out, "tm", -2)
    padded_grad = with_halo(
        jnp.concatenate([grad_out, after_one, after_two], axis=0), (("rows", 1),), 1
    )
    padded = widen_columns(padded)
    padded_grad = widen_columns(padded_grad)
    conv_sum = jnp.zeros((frames_here * rows_here * columns, channels), jnp.float32)
    grad_act = jnp.zeros((frames_here * rows_here * columns, channels), jnp.float32)
    for time_tap in range(3):
        for row_tap in range(3):
            for col_tap in range(3):
                tap_weight = full_weight[time_tap * 9 + row_tap * 3 + col_tap]
                window = padded[
                    time_tap : time_tap + frames_here,
                    row_tap : row_tap + rows_here,
                    col_tap : col_tap + columns,
                ]
                conv_sum = conv_sum + jnp.dot(
                    window.reshape(-1, channels), tap_weight, preferred_element_type=jnp.float32
                )
                back_window = padded_grad[
                    2 - time_tap : 2 - time_tap + frames_here,
                    2 - row_tap : 2 - row_tap + rows_here,
                    2 - col_tap : 2 - col_tap + columns,
                ]
                grad_act = grad_act + lax.dot_general(
                    back_window.reshape(-1, channels),
                    tap_weight,
                    (((1,), (1,)), ((), ())),
                    preferred_element_type=jnp.float32,
                )
    refined = (latent_wide + conv_sum.reshape(latent.shape)).astype(jnp.bfloat16)
    grad_scaled = (
        grad_act.reshape(latent.shape) * sigmoid_value * (1.0 + scaled * (1.0 - sigmoid_value))
    )
    grad_normed = grouped_view(grad_scaled * norm_gain)
    first_sum, second_sum = lax.psum(
        (jnp.sum(grad_normed, axis=(1, 3)), jnp.sum(grad_normed * normed_grouped, axis=(1, 3))),
        "rows",
    )
    first = first_sum / cell_count
    second = second_sum / cell_count
    grad_norm_part = (
        grad_normed - first[:, None, :, None] - normed_grouped * second[:, None, :, None]
    ) * inverse[:, None, :, None]
    grad_latent = grad_out.astype(jnp.float32) + grad_norm_part.reshape(latent.shape)
    return (refined, grad_latent)


def solution(mesh):
    placed = (P("tm", "rows", None, None), P(), P(None, "tm", None), P("tm", "rows", None, None))
    return jax.shard_map(
        shards,
        mesh=mesh,
        in_specs=placed,
        out_specs=(P("tm", "rows", None, None), P("tm", "rows", None, None)),
        check_vma=False,
    )
```

profile of v0, /device:TPU:6, one launch (start us, length us, event | category | flops | bytes accessed | tf_op | source)
XLA Modules:
  0.0 219.8 jit_solution(12708673439425601817)
XLA Ops:
  7.9 1.3 collective-permute-start.4
  11.7 16.1 %psum.28 = f32[1,32]{1,0:T(1,128)S(1)} all-reduce(f32[1,32]{1,0:T(1,128)S(1)} %bitcast.290), channel_id=1, replica_groups=mesh['tm'=32,'rows'=8] {'rows'}, use_global_device_ids=true, to_apply=%region_2.0 | all-reduce | flops 32 | bytes 256 | tf_op jit(solution)/shard_map/psum | solution.py:45
  28.8 5.3 %collective-permute-done.5 = bf16[1,2,128,512]{3,2,1,0:T(8,128)(2,1)S(1)} collective-permute-done((bf16[1,2,128,512]{3,2,1,0:T(8,128)(2,1)}, bf16[1,2,128,512]{3,2,1,0:T(8,128)(2,1)S(1)}, u32[]{:S(2)}, u32[]{:S(2)}) %collective-permute-start.5) | collective-permute-done | bytes 262176 | tf_op jit(solution)/shard_map/ppermute | solution.py:13
  34.9 1.9 collective-permute-start.6
  36.8 3.9 %collective-permute-start.7 = (bf16[3,1,128,512]{3,2,1,0:T(8,128)(2,1)S(1)}, bf16[3,1,128,512]{3,2,1,0:T(8,128)(2,1)S(1)}, u32[]{:S(2)}, u32[]{:S(2)}) collective-permute-start(bf16[3,1,128,512]{3,2,1,0:T(8,128)(2,1)S(1)} %get-tuple-element.59), channel_id=1, source_target_pairs={{1,0},{2,1},{3,2},{4,3},{5,4},{6,5},{7,6},{9,8},{10,9},{11,10},{12... | collective-permute-start | bytes 1179656 | tf_op jit(solution)/shard_map/ppermute | solution.py:24
  42.1 22.3 %psum.29 = f32[1,32]{1,0:T(1,128)S(1)} all-reduce(f32[1,32]{1,0:T(1,128)S(1)} %bitcast.291), channel_id=1, replica_groups=mesh['tm'=32,'rows'=8] {'rows'}, use_global_device_ids=true, to_apply=%region_5.6 | all-reduce | flops 32 | bytes 256 | tf_op jit(solution)/shard_map/psum | solution.py:47
  66.2 1.7 fusion.87
  67.9 52.9 %all-gather.2.cloned.1.call-done = bf16[27,512,512]{2,1,0:T(8,128)(2,1)} async-done(((bf16[27,16,512]{2,1,0:T(8,128)(2,1)}), bf16[27,512,512]{2,1,0:T(8,128)(2,1)}) %all-gather.2.cloned.1.call-update) | async-done | bytes 14155792 | tf_op jit(solution)/shard_map/all_gather | solution.py:42
  120.8 1.6 fusion.59
  122.4 2.1 fusion.41
  124.6 2.2 fusion.77
  126.7 1.4 fusion.53
  128.2 1.5 fusion.35
  129.7 1.5 fusion.71
  131.1 1.5 fusion.81
  132.6 1.4 fusion.65
  134.0 1.4 fusion.47
  135.5 1.5 fusion.79
  137.0 1.5 fusion.33
  145.7 2.3 %collective-permute-start.1 = (bf16[1,2,128,512]{3,2,1,0:T(8,128)(2,1)S(1)}, bf16[1,2,128,512]{3,2,1,0:T(8,128)(2,1)S(1)}, u32[]{:S(2)}, u32[]{:S(2)}) collective-permute-start(bf16[1,2,128,512]{3,2,1,0:T(8,128)(2,1)S(1)} %get-tuple-element.62), channel_id=1, source_target_pairs={{0,8},{8,16},{16,24},{24,32},{32,40},{40,48},{48,56},{56,64},{64,7... | collective-permute-start | bytes 786440 | tf_op jit(solution)/shard_map/ppermute | solution.py:13
  148.0 6.9 %collective-permute-start = (bf16[1,2,128,512]{3,2,1,0:T(8,128)(2,1)S(1)}, bf16[1,2,128,512]{3,2,1,0:T(8,128)(2,1)S(1)}, u32[]{:S(2)}, u32[]{:S(2)}) collective-permute-start(bf16[1,2,128,512]{3,2,1,0:T(8,128)(2,1)S(1)} %get-tuple-element.62), channel_id=1, source_target_pairs={{0,16},{8,24},{16,32},{24,40},{32,48},{40,56},{48,64},{56,72},{64,... | collective-permute-start | bytes 786440 | tf_op jit(solution)/shard_map/ppermute | solution.py:13
  155.2 22.7 %all-reduce.2 = (f32[1,32]{1,0:T(1,128)S(1)}, f32[1,32]{1,0:T(1,128)S(1)}) all-reduce(f32[1,32]{1,0:T(1,128)S(1)} %bitcast.289, f32[1,32]{1,0:T(1,128)S(1)} %bitcast.288), channel_id=1, replica_groups=mesh['tm'=32,'rows'=8] {'rows'}, use_global_device_ids=true, to_apply=%region_11.12 | all-reduce | flops 64 | bytes 512 | tf_op jit(solution)/shard_map/psum | solution.py:96
  178.3 1.3 fusion.78
  179.8 3.7 %collective-permute-start.2 = (bf16[3,1,128,512]{3,2,1,0:T(8,128)(2,1)S(1)}, bf16[3,1,128,512]{3,2,1,0:T(8,128)(2,1)S(1)}, u32[]{:S(2)}, u32[]{:S(2)}) collective-permute-start(bf16[3,1,128,512]{3,2,1,0:T(8,128)(2,1)S(1)} %get-tuple-element.60), channel_id=1, source_target_pairs={{0,1},{1,2},{2,3},{3,4},{4,5},{5,6},{6,7},{8,9},{9,10},{10,11},{11... | collective-permute-start | bytes 1179656 | tf_op jit(solution)/shard_map/ppermute | solution.py:23
  183.6 2.3 %collective-permute-start.3 = (bf16[3,1,128,512]{3,2,1,0:T(8,128)(2,1)S(1)}, bf16[3,1,128,512]{3,2,1,0:T(8,128)(2,1)S(1)}, u32[]{:S(2)}, u32[]{:S(2)}) collective-permute-start(bf16[3,1,128,512]{3,2,1,0:T(8,128)(2,1)S(1)} %get-tuple-element.61), channel_id=1, source_target_pairs={{1,0},{2,1},{3,2},{4,3},{5,4},{6,5},{7,6},{9,8},{10,9},{11,10},{12... | collective-permute-start | bytes 1179656 | tf_op jit(solution)/shard_map/ppermute | solution.py:24
  185.9 1.5 fusion.42
  187.4 1.3 fusion.60
  188.7 4.1 %collective-permute-done.2 = bf16[3,1,128,512]{3,2,1,0:T(8,128)(2,1)S(1)} collective-permute-done((bf16[3,1,128,512]{3,2,1,0:T(8,128)(2,1)S(1)}, bf16[3,1,128,512]{3,2,1,0:T(8,128)(2,1)S(1)}, u32[]{:S(2)}, u32[]{:S(2)}) %collective-permute-start.2) | collective-permute-done | bytes 393248 | tf_op jit(solution)/shard_map/ppermute | solution.py:23
  192.9 5.6 %collective-permute-done.3 = bf16[3,1,128,512]{3,2,1,0:T(8,128)(2,1)S(1)} collective-permute-done((bf16[3,1,128,512]{3,2,1,0:T(8,128)(2,1)S(1)}, bf16[3,1,128,512]{3,2,1,0:T(8,128)(2,1)S(1)}, u32[]{:S(2)}, u32[]{:S(2)}) %collective-permute-start.3) | collective-permute-done | bytes 393248 | tf_op jit(solution)/shard_map/ppermute | solution.py:24
  200.1 1.8 fusion.66
  202.0 1.3 fusion.48
  203.3 1.3 fusion.82
  (107 shorter events, 25.8 us)
Async XLA Ops:
  7.2 117.4 %copy-start.2 = (bf16[1,2,128,512]{3,2,1,0:T(8,128)(2,1)S(1)}, bf16[1,2,128,512]{3,2,1,0:T(8,128)(2,1)}, u32[]{:S(2)}) copy-start(bf16[1,2,128,512]{3,2,1,0:T(8,128)(2,1)} %param.7) | copy-start | bytes 786436
  7.2 113.7 %all-gather.2.cloned.1.call-start = ((), (), s32[]{:S(2)}) async-start(), calls=%async_computation | async-start | bytes 14598144 | tf_op jit(solution)/shard_map/all_gather | solution.py:42
  7.9 20.9 %collective-permute-start.4 = (bf16[1,2,128,512]{3,2,1,0:T(8,128)(2,1)}, bf16[1,2,128,512]{3,2,1,0:T(8,128)(2,1)S(1)}, u32[]{:S(2)}, u32[]{:S(2)}) collective-permute-start(bf16[1,2,128,512]{3,2,1,0:T(8,128)(2,1)} %param.7), channel_id=1, source_target_pairs={{8,0},{16,8},{24,16},{32,24},{40,32},{48,40},{56,48},{64,56},{72,6... | collective-permute-start | bytes 786440 | tf_op jit(solution)/shard_map/ppermute | solution.py:13
  9.2 24.9 %collective-permute-start.5 = (bf16[1,2,128,512]{3,2,1,0:T(8,128)(2,1)}, bf16[1,2,128,512]{3,2,1,0:T(8,128)(2,1)S(1)}, u32[]{:S(2)}, u32[]{:S(2)}) collective-permute-start(bf16[1,2,128,512]{3,2,1,0:T(8,128)(2,1)} %param.7), channel_id=1, source_target_pairs={{16,0},{24,8},{32,16},{40,24},{48,32},{56,40},{64,48},{72,56},{80,... | collective-permute-start | bytes 786440 | tf_op jit(solution)/shard_map/ppermute | solution.py:13
  28.8 5.5 %copy-start.6 = (bf16[1,2,128,512]{3,2,1,0:T(8,128)(2,1)}, bf16[1,2,128,512]{3,2,1,0:T(8,128)(2,1)S(1)}, u32[]{:S(2)}) copy-start(bf16[1,2,128,512]{3,2,1,0:T(8,128)(2,1)S(1)} %collective-permute-done.4) | copy-start | bytes 786436
  34.2 0.7 copy-start.7
  34.9 29.8 %collective-permute-start.6 = (bf16[3,1,128,512]{3,2,1,0:T(8,128)(2,1)S(1)}, bf16[3,1,128,512]{3,2,1,0:T(8,128)(2,1)S(1)}, u32[]{:S(2)}, u32[]{:S(2)}) collective-permute-start(bf16[3,1,128,512]{3,2,1,0:T(8,128)(2,1)S(1)} %get-tuple-element.58), channel_id=1, source_target_pairs={{0,1},{1,2},{2,3},{3,4},{4,5},{5,6},{6,7},{8,9},{9,10},{10,11},{11... | collective-permute-start | bytes 1179656 | tf_op jit(solution)/shard_map/ppermute | solution.py:23
  36.8 27.9 %collective-permute-start.7 = (bf16[3,1,128,512]{3,2,1,0:T(8,128)(2,1)S(1)}, bf16[3,1,128,512]{3,2,1,0:T(8,128)(2,1)S(1)}, u32[]{:S(2)}, u32[]{:S(2)}) collective-permute-start(bf16[3,1,128,512]{3,2,1,0:T(8,128)(2,1)S(1)} %get-tuple-element.59), channel_id=1, source_target_pairs={{1,0},{2,1},{3,2},{4,3},{5,4},{6,5},{7,6},{9,8},{10,9},{11,10},{12... | collective-permute-start | bytes 1179656 | tf_op jit(solution)/shard_map/ppermute | solution.py:24
  120.8 17.6 %copy-start = (bf16[27,512,512]{2,1,0:T(8,128)(2,1)S(1)}, bf16[27,512,512]{2,1,0:T(8,128)(2,1)}, u32[]{:S(2)}) copy-start(bf16[27,512,512]{2,1,0:T(8,128)(2,1)} %all-gather.2.cloned.1.call-done) | copy-start | bytes 42467332
  120.8 18.9 %copy-start.5 = (bf16[1,2,128,512]{3,2,1,0:T(8,128)(2,1)S(1)}, bf16[1,2,128,512]{3,2,1,0:T(8,128)(2,1)}, u32[]{:S(2)}) copy-start(bf16[1,2,128,512]{3,2,1,0:T(8,128)(2,1)} %get-tuple-element.11) | copy-start | bytes 786436
  120.8 19.2 %copy-start.4 = (bf16[1,2,128,512]{3,2,1,0:T(8,128)(2,1)S(1)}, bf16[1,2,128,512]{3,2,1,0:T(8,128)(2,1)}, u32[]{:S(2)}) copy-start(bf16[1,2,128,512]{3,2,1,0:T(8,128)(2,1)} %get-tuple-element.12) | copy-start | bytes 786436
  120.8 19.6 %copy-start.3 = (bf16[1,2,128,512]{3,2,1,0:T(8,128)(2,1)S(1)}, bf16[1,2,128,512]{3,2,1,0:T(8,128)(2,1)}, u32[]{:S(2)}) copy-start(bf16[1,2,128,512]{3,2,1,0:T(8,128)(2,1)} %get-tuple-element.13) | copy-start | bytes 786436
  141.1 4.2 %copy-start.1 = (bf16[1,2,128,512]{3,2,1,0:T(8,128)(2,1)S(1)}, bf16[1,2,128,512]{3,2,1,0:T(8,128)(2,1)}, u32[]{:S(2)}) copy-start(bf16[1,2,128,512]{3,2,1,0:T(8,128)(2,1)} %param.4) | copy-start | bytes 786436
  141.1 4.2 %copy-start.8 = (f32[512]{0:T(512)S(1)}, f32[512]{0:T(512)}, u32[]{:S(2)}) copy-start(f32[512]{0:T(512)} %param.5) | copy-start | bytes 6148
  145.3 59.3 %slice-start = ((s8[14155776]{0:T(1024)(128)(4,1)}), s8[1572864]{0:T(1024)(128)(4,1)S(1)}, s32[]{:S(2)}) async-start(s8[14155776]{0:T(1024)(128)(4,1)} %bitcast.231), calls=%async_computation.1 | async-start | bytes 3145728
  145.7 34.0 %collective-permute-start.1 = (bf16[1,2,128,512]{3,2,1,0:T(8,128)(2,1)S(1)}, bf16[1,2,128,512]{3,2,1,0:T(8,128)(2,1)S(1)}, u32[]{:S(2)}, u32[]{:S(2)}) collective-permute-start(bf16[1,2,128,512]{3,2,1,0:T(8,128)(2,1)S(1)} %get-tuple-element.62), channel_id=1, source_target_pairs={{0,8},{8,16},{16,24},{24,32},{32,40},{40,48},{48,56},{56,64},{64,7... | collective-permute-start | bytes 786440 | tf_op jit(solution)/shard_map/ppermute | solution.py:13
  148.0 31.7 %collective-permute-start = (bf16[1,2,128,512]{3,2,1,0:T(8,128)(2,1)S(1)}, bf16[1,2,128,512]{3,2,1,0:T(8,128)(2,1)S(1)}, u32[]{:S(2)}, u32[]{:S(2)}) collective-permute-start(bf16[1,2,128,512]{3,2,1,0:T(8,128)(2,1)S(1)} %get-tuple-element.62), channel_id=1, source_target_pairs={{0,16},{8,24},{16,32},{24,40},{32,48},{40,56},{48,64},{56,72},{64,... | collective-permute-start | bytes 786440 | tf_op jit(solution)/shard_map/ppermute | solution.py:13
  179.8 13.0 %collective-permute-start.2 = (bf16[3,1,128,512]{3,2,1,0:T(8,128)(2,1)S(1)}, bf16[3,1,128,512]{3,2,1,0:T(8,128)(2,1)S(1)}, u32[]{:S(2)}, u32[]{:S(2)}) collective-permute-start(bf16[3,1,128,512]{3,2,1,0:T(8,128)(2,1)S(1)} %get-tuple-element.60), channel_id=1, source_target_pairs={{0,1},{1,2},{2,3},{3,4},{4,5},{5,6},{6,7},{8,9},{9,10},{10,11},{11... | collective-permute-start | bytes 1179656 | tf_op jit(solution)/shard_map/ppermute | solution.py:23
  183.6 14.8 %collective-permute-start.3 = (bf16[3,1,128,512]{3,2,1,0:T(8,128)(2,1)S(1)}, bf16[3,1,128,512]{3,2,1,0:T(8,128)(2,1)S(1)}, u32[]{:S(2)}, u32[]{:S(2)}) collective-permute-start(bf16[3,1,128,512]{3,2,1,0:T(8,128)(2,1)S(1)} %get-tuple-element.61), channel_id=1, source_target_pairs={{1,0},{2,1},{3,2},{4,3},{5,4},{6,5},{7,6},{9,8},{10,9},{11,10},{12... | collective-permute-start | bytes 1179656 | tf_op jit(solution)/shard_map/ppermute | solution.py:24
  185.9 18.8 %slice-start.1 = ((s8[14155776]{0:T(1024)(128)(4,1)}), s8[4194304]{0:T(1024)(128)(4,1)S(1)}, s32[]{:S(2)}) async-start(s8[14155776]{0:T(1024)(128)(4,1)} %bitcast.231), calls=%async_computation.2 | async-start | bytes 8388608
  199.2 5.5 %slice-start.2 = ((s8[14155776]{0:T(1024)(128)(4,1)}), s8[4194304]{0:T(1024)(128)(4,1)S(1)}, s32[]{:S(2)}) async-start(s8[14155776]{0:T(1024)(128)(4,1)} %bitcast.231), calls=%async_computation.3 | async-start | bytes 8388608
  199.9 4.7 %slice-start.3 = ((s8[14155776]{0:T(1024)(128)(4,1)}), s8[4194304]{0:T(1024)(128)(4,1)S(1)}, s32[]{:S(2)}) async-start(s8[14155776]{0:T(1024)(128)(4,1)} %bitcast.231), calls=%async_computation.4 | async-start | bytes 8388608
Sparse Core Ops, SparseCore 0:
  10.6 110.1 all-gather.1
where the time goes:
time: 221 us; the launch traced here: 220 us
  waiting for transfers between devices  68.6 us (31%)
  blocking collectives  61.2 us (28%)
  matrix products  39.8 us (18%)
  starting transfers between devices  23.6 us (11%)
  between operations  14.8 us (7%)
  other arithmetic  6.57 us (3%)
  local copies, waits for them, and re-layouts  5.16 us (2%)
    all_gather x1, waiting for transfers between devices, shards(): full_weight = lax.all_gather(conv_weight, 'tm', axis=1, tiled=True)  52.9 us
    dot_general x27, matrix products, shards(): lax.dot_general(back_window.reshape(-1, channels), tap_weight, (((1,), (1...  24.2 us
    psum x1, blocking collectives, shards(): lax.psum((jnp.sum(grad_normed, axis=(1, 3)), jnp.sum(grad_normed * normed...  22.7 us
    psum x1, blocking collectives, shards(): lax.psum(jnp.sum(centred * centred, axis=(1, 3)), 'rows') / cell_count  22.3 us
    psum x1, blocking collectives, shards(): average = lax.psum(jnp.sum(grouped, axis=(1, 3)), 'rows') / cell_count  16.1 us
    dot_general x27, matrix products, shards(): jnp.dot(window.reshape(-1, channels), tap_weight, preferred_element_type=...  15.7 us
    ppermute x4, starting transfers between devices, shifted(): return lax.ppermute(block, axis, route)  11.8 us
    ppermute x2, starting transfers between devices, with_halo(): after = lax.ppermute(first, axis, down)  6.21 us
  transfers between devices with their start and end apart: 9, of which 4 were waited for; matrix products, arithmetic and copies ran while one was open for 5% of the time, Pallas kernels for 0%

commit v1 on v0

--- a/solution.py
+++ b/solution.py
@@ -42,7 +42,7 @@
     full_weight = lax.all_gather(conv_weight, "tm", axis=1, tiled=True)
     latent_wide = latent.astype(jnp.float32)
     grouped = grouped_view(latent_wide)
-    average = lax.psum(jnp.sum(grouped, axis=(1, 3)), "rows") / cell_count
+    average = jnp.sum(lax.all_gather(jnp.sum(grouped, axis=(1, 3)), "rows"), axis=0) / cell_count
     centred = grouped - average[:, None, :, None]
     spread = lax.psum(jnp.sum(centred * centred, axis=(1, 3)), "rows") / cell_count
     inverse = lax.rsqrt(spread + epsilon)

time: 221 us -> 220 us (level)
  starting transfers between devices: 23.6 us -> 21.1 us
    unnamed x0 -> x1, blocking collectives: none -> 16.4 us
    psum x1 -> x0, blocking collectives: 16.1 us -> none  [shards(): average = lax.psum(jnp.sum(grouped, axis=(1, 3)), 'rows') / cell_count]
    ppermute x4, starting transfers between devices: 11.8 us -> 8.31 us  [shifted(): return lax.ppermute(block, axis, route)]
    all_gather x1, waiting for transfers between devices: 52.9 us -> 56 us  [shards(): full_weight = lax.all_gather(conv_weight, 'tm', axis=1, tiled=True)]
    ppermute x4, waiting for transfers between devices: 5.33 us -> 2.72 us  [shifted(): return lax.ppermute(block, axis, route)]
  transfers between devices with their start and end apart: 9 -> 9, of which waited for: 4 -> 4; matrix products, arithmetic and copies ran while one was open for 5% -> 6% of each run, Pallas kernels for 0% -> 0%
where the time goes in v1:
time: 220 us; the launch traced here: 219 us
  waiting for transfers between devices  68.5 us (31%)
  blocking collectives  60.8 us (28%)
  matrix products  39.8 us (18%)
  starting transfers between devices  21.1 us (10%)
  between operations  15.5 us (7%)
  local copies, waits for them, and re-layouts  6.74 us (3%)
  other arithmetic  6.58 us (3%)
    all_gather x1, waiting for transfers between devices, shards(): full_weight = lax.all_gather(conv_weight, 'tm', axis=1, tiled=True)  56 us
    dot_general x27, matrix products, shards(): lax.dot_general(back_window.reshape(-1, channels), tap_weight, (((1,), (1...  24.2 us
    psum x1, blocking collectives, shards(): lax.psum(jnp.sum(centred * centred, axis=(1, 3)), 'rows') / cell_count  22.5 us
    psum x1, blocking collectives, shards(): lax.psum((jnp.sum(grad_normed, axis=(1, 3)), jnp.sum(grad_normed * normed...  21.9 us
    unnamed x1, blocking collectives  16.4 us
    dot_general x27, matrix products, shards(): jnp.dot(window.reshape(-1, channels), tap_weight, preferred_element_type=...  15.7 us
    ppermute x4, starting transfers between devices, shifted(): return lax.ppermute(block, axis, route)  8.31 us
    ppermute x2, starting transfers between devices, with_halo(): before = lax.ppermute(last, axis, up)  7.79 us
  transfers between devices with their start and end apart: 9, of which 4 were waited for; matrix products, arithmetic and copies ran while one was open for 6% of the time, Pallas kernels for 0%

profile of v1, /device:TPU:6, one launch (start us, length us, event | category | flops | bytes accessed | tf_op | source)
XLA Modules:
  0.0 219.0 jit_solution(14112690406929366861)
XLA Ops:
  7.9 1.3 collective-permute-start.4
  13.9 16.4 %all-reduce.2 = f32[256]{0:T(256)S(1)} all-reduce(f32[256]{0:T(256)S(1)} %dynamic-update-slice), channel_id=2, replica_groups=mesh['tm'=32,'rows'=8] {'rows'}, use_global_device_ids=true, to_apply=%add.2 | all-reduce | flops 256 | bytes 2048
  31.4 2.7 %collective-permute-done.5 = bf16[1,2,128,512]{3,2,1,0:T(8,128)(2,1)S(1)} collective-permute-done((bf16[1,2,128,512]{3,2,1,0:T(8,128)(2,1)}, bf16[1,2,128,512]{3,2,1,0:T(8,128)(2,1)S(1)}, u32[]{:S(2)}, u32[]{:S(2)}) %collective-permute-start.5) | collective-permute-done | bytes 262176 | tf_op jit(solution)/shard_map/ppermute | solution.py:13
  34.9 4.0 %collective-permute-start.6 = (bf16[3,1,128,512]{3,2,1,0:T(8,128)(2,1)S(1)}, bf16[3,1,128,512]{3,2,1,0:T(8,128)(2,1)S(1)}, u32[]{:S(2)}, u32[]{:S(2)}) collective-permute-start(bf16[3,1,128,512]{3,2,1,0:T(8,128)(2,1)S(1)} %get-tuple-element.58), channel_id=1, source_target_pairs={{0,1},{1,2},{2,3},{3,4},{4,5},{5,6},{6,7},{8,9},{9,10},{10,11},{11... | collective-permute-start | bytes 1179656 | tf_op jit(solution)/shard_map/ppermute | solution.py:23
  38.9 1.9 collective-permute-start.7
  42.2 22.5 %psum.21 = f32[1,32]{1,0:T(1,128)S(1)} all-reduce(f32[1,32]{1,0:T(1,128)S(1)} %bitcast.288), channel_id=1, replica_groups=mesh['tm'=32,'rows'=8] {'rows'}, use_global_device_ids=true, to_apply=%region_5.6 | all-reduce | flops 32 | bytes 256 | tf_op jit(solution)/shard_map/psum | solution.py:47
  66.5 1.7 fusion.87
  68.2 56.0 %all-gather.3.cloned.1.call-done = bf16[27,512,512]{2,1,0:T(8,128)(2,1)} async-done(((bf16[27,16,512]{2,1,0:T(8,128)(2,1)}), bf16[27,512,512]{2,1,0:T(8,128)(2,1)}) %all-gather.3.cloned.1.call-update) | async-done | bytes 14155792 | tf_op jit(solution)/shard_map/all_gather | solution.py:42
  124.2 1.6 fusion.59
  125.8 2.1 fusion.41
  127.9 2.2 fusion.77
  130.1 1.5 fusion.53
  131.5 1.4 fusion.35
  133.0 1.4 fusion.71
  134.4 1.4 fusion.81
  135.9 1.4 fusion.65
  137.3 1.4 fusion.47
  138.8 1.5 fusion.79
  140.3 1.5 fusion.33
  149.0 2.3 %collective-permute-start.1 = (bf16[1,2,128,512]{3,2,1,0:T(8,128)(2,1)S(1)}, bf16[1,2,128,512]{3,2,1,0:T(8,128)(2,1)S(1)}, u32[]{:S(2)}, u32[]{:S(2)}) collective-permute-start(bf16[1,2,128,512]{3,2,1,0:T(8,128)(2,1)S(1)} %get-tuple-element.62), channel_id=1, source_target_pairs={{0,8},{8,16},{16,24},{24,32},{32,40},{40,48},{48,56},{56,64},{64,7... | collective-permute-start | bytes 786440 | tf_op jit(solution)/shard_map/ppermute | solution.py:13
  151.3 3.4 %collective-permute-start = (bf16[1,2,128,512]{3,2,1,0:T(8,128)(2,1)S(1)}, bf16[1,2,128,512]{3,2,1,0:T(8,128)(2,1)S(1)}, u32[]{:S(2)}, u32[]{:S(2)}) collective-permute-start(bf16[1,2,128,512]{3,2,1,0:T(8,128)(2,1)S(1)} %get-tuple-element.62), channel_id=1, source_target_pairs={{0,16},{8,24},{16,32},{24,40},{32,48},{40,56},{48,64},{56,72},{64,... | collective-permute-start | bytes 786440 | tf_op jit(solution)/shard_map/ppermute | solution.py:13
  155.1 21.9 %all-reduce.3 = (f32[1,32]{1,0:T(1,128)S(1)}, f32[1,32]{1,0:T(1,128)S(1)}) all-reduce(f32[1,32]{1,0:T(1,128)S(1)} %bitcast.287, f32[1,32]{1,0:T(1,128)S(1)} %bitcast.286), channel_id=1, replica_groups=mesh['tm'=32,'rows'=8] {'rows'}, use_global_device_ids=true, to_apply=%region_11.12 | all-reduce | flops 64 | bytes 512 | tf_op jit(solution)/shard_map/psum | solution.py:96
  177.3 1.3 fusion.78
  178.9 3.8 %collective-permute-start.2 = (bf16[3,1,128,512]{3,2,1,0:T(8,128)(2,1)S(1)}, bf16[3,1,128,512]{3,2,1,0:T(8,128)(2,1)S(1)}, u32[]{:S(2)}, u32[]{:S(2)}) collective-permute-start(bf16[3,1,128,512]{3,2,1,0:T(8,128)(2,1)S(1)} %get-tuple-element.60), channel_id=1, source_target_pairs={{0,1},{1,2},{2,3},{3,4},{4,5},{5,6},{6,7},{8,9},{9,10},{10,11},{11... | collective-permute-start | bytes 1179656 | tf_op jit(solution)/shard_map/ppermute | solution.py:23
  182.6 3.0 %collective-permute-start.3 = (bf16[3,1,128,512]{3,2,1,0:T(8,128)(2,1)S(1)}, bf16[3,1,128,512]{3,2,1,0:T(8,128)(2,1)S(1)}, u32[]{:S(2)}, u32[]{:S(2)}) collective-permute-start(bf16[3,1,128,512]{3,2,1,0:T(8,128)(2,1)S(1)} %get-tuple-element.61), channel_id=1, source_target_pairs={{1,0},{2,1},{3,2},{4,3},{5,4},{6,5},{7,6},{9,8},{10,9},{11,10},{12... | collective-permute-start | bytes 1179656 | tf_op jit(solution)/shard_map/ppermute | solution.py:24
  185.7 1.5 fusion.42
  187.2 1.3 fusion.60
  188.5 3.4 %collective-permute-done.2 = bf16[3,1,128,512]{3,2,1,0:T(8,128)(2,1)S(1)} collective-permute-done((bf16[3,1,128,512]{3,2,1,0:T(8,128)(2,1)S(1)}, bf16[3,1,128,512]{3,2,1,0:T(8,128)(2,1)S(1)}, u32[]{:S(2)}, u32[]{:S(2)}) %collective-permute-start.2) | collective-permute-done | bytes 393248 | tf_op jit(solution)/shard_map/ppermute | solution.py:23
  191.9 5.8 %collective-permute-done.3 = bf16[3,1,128,512]{3,2,1,0:T(8,128)(2,1)S(1)} collective-permute-done((bf16[3,1,128,512]{3,2,1,0:T(8,128)(2,1)S(1)}, bf16[3,1,128,512]{3,2,1,0:T(8,128)(2,1)S(1)}, u32[]{:S(2)}, u32[]{:S(2)}) %collective-permute-start.3) | collective-permute-done | bytes 393248 | tf_op jit(solution)/shard_map/ppermute | solution.py:24
  199.4 1.8 fusion.66
  201.2 1.3 fusion.48
  202.5 1.3 fusion.82
  (112 shorter events, 27.4 us)
Async XLA Ops:
  7.2 120.7 %copy-start.2 = (bf16[1,2,128,512]{3,2,1,0:T(8,128)(2,1)S(1)}, bf16[1,2,128,512]{3,2,1,0:T(8,128)(2,1)}, u32[]{:S(2)}) copy-start(bf16[1,2,128,512]{3,2,1,0:T(8,128)(2,1)} %param.7) | copy-start | bytes 786436
  7.2 117.0 %all-gather.3.cloned.1.call-start = ((), (), s32[]{:S(2)}) async-start(), calls=%async_computation | async-start | bytes 14598144 | tf_op jit(solution)/shard_map/all_gather | solution.py:42
  7.9 23.5 %collective-permute-start.4 = (bf16[1,2,128,512]{3,2,1,0:T(8,128)(2,1)}, bf16[1,2,128,512]{3,2,1,0:T(8,128)(2,1)S(1)}, u32[]{:S(2)}, u32[]{:S(2)}) collective-permute-start(bf16[1,2,128,512]{3,2,1,0:T(8,128)(2,1)} %param.7), channel_id=1, source_target_pairs={{8,0},{16,8},{24,16},{32,24},{40,32},{48,40},{56,48},{64,56},{72,6... | collective-permute-start | bytes 786440 | tf_op jit(solution)/shard_map/ppermute | solution.py:13
  9.2 24.9 %collective-permute-start.5 = (bf16[1,2,128,512]{3,2,1,0:T(8,128)(2,1)}, bf16[1,2,128,512]{3,2,1,0:T(8,128)(2,1)S(1)}, u32[]{:S(2)}, u32[]{:S(2)}) collective-permute-start(bf16[1,2,128,512]{3,2,1,0:T(8,128)(2,1)} %param.7), channel_id=1, source_target_pairs={{16,0},{24,8},{32,16},{40,24},{48,32},{56,40},{64,48},{72,56},{80,... | collective-permute-start | bytes 786440 | tf_op jit(solution)/shard_map/ppermute | solution.py:13
  31.4 2.9 %copy-start.6 = (bf16[1,2,128,512]{3,2,1,0:T(8,128)(2,1)}, bf16[1,2,128,512]{3,2,1,0:T(8,128)(2,1)S(1)}, u32[]{:S(2)}) copy-start(bf16[1,2,128,512]{3,2,1,0:T(8,128)(2,1)S(1)} %collective-permute-done.4) | copy-start | bytes 786436
  34.2 0.7 copy-start.7
  34.9 30.1 %collective-permute-start.6 = (bf16[3,1,128,512]{3,2,1,0:T(8,128)(2,1)S(1)}, bf16[3,1,128,512]{3,2,1,0:T(8,128)(2,1)S(1)}, u32[]{:S(2)}, u32[]{:S(2)}) collective-permute-start(bf16[3,1,128,512]{3,2,1,0:T(8,128)(2,1)S(1)} %get-tuple-element.58), channel_id=1, source_target_pairs={{0,1},{1,2},{2,3},{3,4},{4,5},{5,6},{6,7},{8,9},{9,10},{10,11},{11... | collective-permute-start | bytes 1179656 | tf_op jit(solution)/shard_map/ppermute | solution.py:23
  38.9 26.0 %collective-permute-start.7 = (bf16[3,1,128,512]{3,2,1,0:T(8,128)(2,1)S(1)}, bf16[3,1,128,512]{3,2,1,0:T(8,128)(2,1)S(1)}, u32[]{:S(2)}, u32[]{:S(2)}) collective-permute-start(bf16[3,1,128,512]{3,2,1,0:T(8,128)(2,1)S(1)} %get-tuple-element.59), channel_id=1, source_target_pairs={{1,0},{2,1},{3,2},{4,3},{5,4},{6,5},{7,6},{9,8},{10,9},{11,10},{12... | collective-permute-start | bytes 1179656 | tf_op jit(solution)/shard_map/ppermute | solution.py:24
  124.1 17.6 %copy-start = (bf16[27,512,512]{2,1,0:T(8,128)(2,1)S(1)}, bf16[27,512,512]{2,1,0:T(8,128)(2,1)}, u32[]{:S(2)}) copy-start(bf16[27,512,512]{2,1,0:T(8,128)(2,1)} %all-gather.3.cloned.1.call-done) | copy-start | bytes 42467332
  124.1 18.9 %copy-start.5 = (bf16[1,2,128,512]{3,2,1,0:T(8,128)(2,1)S(1)}, bf16[1,2,128,512]{3,2,1,0:T(8,128)(2,1)}, u32[]{:S(2)}) copy-start(bf16[1,2,128,512]{3,2,1,0:T(8,128)(2,1)} %get-tuple-element.11) | copy-start | bytes 786436
  124.2 19.2 %copy-start.4 = (bf16[1,2,128,512]{3,2,1,0:T(8,128)(2,1)S(1)}, bf16[1,2,128,512]{3,2,1,0:T(8,128)(2,1)}, u32[]{:S(2)}) copy-start(bf16[1,2,128,512]{3,2,1,0:T(8,128)(2,1)} %get-tuple-element.12) | copy-start | bytes 786436
  124.2 19.6 %copy-start.3 = (bf16[1,2,128,512]{3,2,1,0:T(8,128)(2,1)S(1)}, bf16[1,2,128,512]{3,2,1,0:T(8,128)(2,1)}, u32[]{:S(2)}) copy-start(bf16[1,2,128,512]{3,2,1,0:T(8,128)(2,1)} %get-tuple-element.13) | copy-start | bytes 786436
  144.4 4.2 %copy-start.1 = (bf16[1,2,128,512]{3,2,1,0:T(8,128)(2,1)S(1)}, bf16[1,2,128,512]{3,2,1,0:T(8,128)(2,1)}, u32[]{:S(2)}) copy-start(bf16[1,2,128,512]{3,2,1,0:T(8,128)(2,1)} %param.4) | copy-start | bytes 786436
  144.4 4.2 %copy-start.8 = (f32[512]{0:T(512)S(1)}, f32[512]{0:T(512)}, u32[]{:S(2)}) copy-start(f32[512]{0:T(512)} %param.5) | copy-start | bytes 6148
  148.6 55.2 %slice-start = ((s8[14155776]{0:T(1024)(128)(4,1)}), s8[1572864]{0:T(1024)(128)(4,1)S(1)}, s32[]{:S(2)}) async-start(s8[14155776]{0:T(1024)(128)(4,1)} %bitcast.229), calls=%async_computation.1 | async-start | bytes 3145728
  149.0 29.7 %collective-permute-start.1 = (bf16[1,2,128,512]{3,2,1,0:T(8,128)(2,1)S(1)}, bf16[1,2,128,512]{3,2,1,0:T(8,128)(2,1)S(1)}, u32[]{:S(2)}, u32[]{:S(2)}) collective-permute-start(bf16[1,2,128,512]{3,2,1,0:T(8,128)(2,1)S(1)} %get-tuple-element.62), channel_id=1, source_target_pairs={{0,8},{8,16},{16,24},{24,32},{32,40},{40,48},{48,56},{56,64},{64,7... | collective-permute-start | bytes 786440 | tf_op jit(solution)/shard_map/ppermute | solution.py:13
  151.3 27.4 %collective-permute-start = (bf16[1,2,128,512]{3,2,1,0:T(8,128)(2,1)S(1)}, bf16[1,2,128,512]{3,2,1,0:T(8,128)(2,1)S(1)}, u32[]{:S(2)}, u32[]{:S(2)}) collective-permute-start(bf16[1,2,128,512]{3,2,1,0:T(8,128)(2,1)S(1)} %get-tuple-element.62), channel_id=1, source_target_pairs={{0,16},{8,24},{16,32},{24,40},{32,48},{40,56},{48,64},{56,72},{64,... | collective-permute-start | bytes 786440 | tf_op jit(solution)/shard_map/ppermute | solution.py:13
  178.9 13.0 %collective-permute-start.2 = (bf16[3,1,128,512]{3,2,1,0:T(8,128)(2,1)S(1)}, bf16[3,1,128,512]{3,2,1,0:T(8,128)(2,1)S(1)}, u32[]{:S(2)}, u32[]{:S(2)}) collective-permute-start(bf16[3,1,128,512]{3,2,1,0:T(8,128)(2,1)S(1)} %get-tuple-element.60), channel_id=1, source_target_pairs={{0,1},{1,2},{2,3},{3,4},{4,5},{5,6},{6,7},{8,9},{9,10},{10,11},{11... | collective-permute-start | bytes 1179656 | tf_op jit(solution)/shard_map/ppermute | solution.py:23
  182.6 15.0 %collective-permute-start.3 = (bf16[3,1,128,512]{3,2,1,0:T(8,128)(2,1)S(1)}, bf16[3,1,128,512]{3,2,1,0:T(8,128)(2,1)S(1)}, u32[]{:S(2)}, u32[]{:S(2)}) collective-permute-start(bf16[3,1,128,512]{3,2,1,0:T(8,128)(2,1)S(1)} %get-tuple-element.61), channel_id=1, source_target_pairs={{1,0},{2,1},{3,2},{4,3},{5,4},{6,5},{7,6},{9,8},{10,9},{11,10},{12... | collective-permute-start | bytes 1179656 | tf_op jit(solution)/shard_map/ppermute | solution.py:24
  185.7 18.2 %slice-start.1 = ((s8[14155776]{0:T(1024)(128)(4,1)}), s8[4194304]{0:T(1024)(128)(4,1)S(1)}, s32[]{:S(2)}) async-start(s8[14155776]{0:T(1024)(128)(4,1)} %bitcast.229), calls=%async_computation.2 | async-start | bytes 8388608
  198.4 5.5 %slice-start.2 = ((s8[14155776]{0:T(1024)(128)(4,1)}), s8[4194304]{0:T(1024)(128)(4,1)S(1)}, s32[]{:S(2)}) async-start(s8[14155776]{0:T(1024)(128)(4,1)} %bitcast.229), calls=%async_computation.3 | async-start | bytes 8388608
  199.2 4.7 %slice-start.3 = ((s8[14155776]{0:T(1024)(128)(4,1)}), s8[4194304]{0:T(1024)(128)(4,1)S(1)}, s32[]{:S(2)}) async-start(s8[14155776]{0:T(1024)(128)(4,1)} %bitcast.229), calls=%async_computation.4 | async-start | bytes 8388608
Sparse Core Ops, SparseCore 0:
  10.6 113.4 all-gather.2
